TPU v7x, 32 devices: a whole 2x2x4 slice. The times are simulated.
32 devices in a mesh: row: 4 (over y, x), col: 8 (over z, core).
Axes of the slice: x: 2, y: 2, z: 4, core: 2. Of those that a mesh axis runs over, the one named last changes fastest.
Arguments:
- sensitivity: bfloat16 [8192, 8, 4096], P('row', None, 'col'), may hold values from -0.25 to 0.25
- sample_weight: float32 [8192], P('row'), may hold values from 0.2 to 5
- pattern: int32 [16, 8, 8], P('row', None, 'col'), may hold values 0 or 1
- prior: float32 [2048], P('row'), may hold values from 0.5 to 5
Outputs:
- factored_band: float32 [2048, 8, 4096], P('row', None, 'col')
Inputs may be any that keep to these rules, and one draw needn't show every extreme that they name: pattern holds only 0 and 1.
All inputs are finite; a program needn't handle non-finite values. No bound on the sum of `pattern` on one device may be relied on, other than what follows from the above.
Results may differ from a plain program's by a relative error of at most 0.0028.
Values may be sent and summed in bfloat16 or wider, within the bound.
No kernel may reach another device: no remote copies, remote signals or barrier semaphores. Data moves between devices by JAX's collectives and lax.ppermute only.
A program may use at most 128 MiB of HBM per device.

v0:
```python
import jax
import jax.numpy as jnp
from jax import lax
from jax.sharding import PartitionSpec as P


def spread(value, axis, root):
    mine = lax.axis_index(axis) == root
    return lax.psum(jnp.where(mine, value, jnp.zeros_like(value)), axis)


def body(sensitivity, sample_weight, pattern, prior):
    rows_here = sensitivity.shape[0]
    cycles = sensitivity.shape[1]
    tile = sensitivity.shape[2]
    blocks = pattern.shape[0]
    widths = cycles * tile
    mask_blocks = pattern.astype(jnp.bfloat16)[:, None, :, :]
    masked = (sensitivity.reshape(blocks, tile, cycles, tile) * mask_blocks).reshape(
        rows_here, widths
    )
    weighted = (sample_weight[:, None] * masked.astype(jnp.float32)).astype(jnp.bfloat16)
    first_tile = masked[:, :tile]
    row_count = lax.axis_size("row")
    band_parts = []
    for owner in range(row_count):
        band_parts.append(spread(first_tile, "col", owner))
    band = jnp.concatenate(band_parts, axis=1)
    band_weighted = (sample_weight[:, None] * band.astype(jnp.float32)).astype(jnp.bfloat16)
    head = lax.psum(
        jnp.einsum("sb,sc->bc", band[:, :tile], band_weighted, preferred_element_type=jnp.float32),
        "row",
    )
    prior_head = lax.all_gather(prior, "row", tiled=True)[:tile]
    identity = jnp.eye(tile, dtype=jnp.float32)
    corner = head[:, :tile] + identity * prior_head[None, :]
    lower = jnp.linalg.cholesky(corner)
    lower_inv = jax.scipy.linalg.solve_triangular(lower, identity, lower=True)
    hi = lax.Precision.HIGHEST
    side_panel = jnp.dot(lower_inv, head[:, tile:], precision=hi)
    side_t = jnp.dot(side_panel.T, lower_inv, precision=hi)
    transform = jnp.concatenate([lower_inv, -side_t], axis=0)
    part_head = jnp.einsum(
        "sb,sc->bc", band[:, :tile], weighted, preferred_element_type=jnp.float32
    )
    part_rest = jnp.einsum(
        "sb,sc->bc", band[:, tile:], weighted, preferred_element_type=jnp.float32
    )
    moved = jnp.dot(transform, part_head, precision=lax.Precision.HIGH)
    partial = moved + jnp.concatenate([jnp.zeros((tile, widths), jnp.float32), part_rest], axis=0)
    result = lax.psum_scatter(partial, "row", scatter_dimension=0, tiled=True)
    row = lax.axis_index("row")
    col = lax.axis_index("col")
    mine = lax.dynamic_slice_in_dim(transform, row * tile, tile, axis=0)
    head_on = (col == 0).astype(jnp.float32)
    diag_on = ((col == row) & (row != 0)).astype(jnp.float32)
    fix = head_on * mine * prior_head[None, :] + diag_on * identity * prior[None, :]
    result = result.at[:, :tile].add(fix)
    return result.reshape(tile, cycles, tile)


def solution(mesh):
    return jax.shard_map(
        body,
        mesh=mesh,
        in_specs=(P("row", None, "col"), P("row"), P("row", None, "col"), P("row")),
        out_specs=P("row", None, "col"),
        check_vma=False,
    )
```

profile of v0, /device:TPU:0, one launch (start us, length us, event | category | flops | bytes accessed | tf_op | source)
XLA Modules:
  0.0 846.0 jit_solution(15876469855539642256)
XLA Ops:
  7.2 1.7 mul.67
  9.0 6.3 copy.50
  15.2 12.2 %copy.49 = bf16[256,8,8,512]{3,1,2,0:T(8,128)(2,1)S(1)} copy(bf16[256,8,8,512]{3,2,1,0:T(8,128)(2,1)} %bitcast.65) | data formatting | bytes 33554432
  27.4 9.4 %mul.69 = bf16[2048,4096]{1,0:T(8,128)(2,1)} multiply(bf16[2048,4096]{1,0:T(8,128)(2,1)S(1)} %bitcast.63, bf16[2048,4096]{1,0:T(8,128)(2,1)S(1)} %bitcast.62) | non-fusion elementwise | flops 8388608 | bytes 50331648 | tf_op jit(solution)/shard_map/mul | solution.py:19
  36.8 5.1 broadcast_select_fusion.3
  42.5 9.6 %all-gather = f32[4,1,512]{2,1,0:T(1,128)S(1)} all-gather(f32[1,1,512]{2,1,0:T(1,128)S(1)} %bitcast.70), channel_id=1, replica_groups=mesh['row'=4,'col'=8] {'row'}, dimensions={0}, use_global_device_ids=true | all-gather | bytes 10240 | tf_op jit(solution)/shard_map/all_gather | solution.py:34
  52.3 168.0 %all-reduce.8.cloned.1.call-done = (bf16[2048,512]{1,0:T(8,128)(2,1)}, bf16[2048,512]{1,0:T(8,128)(2,1)}, bf16[2048,512]{1,0:T(8,128)(2,1)}, bf16[2048,512]{1,0:T(8,128)(2,1)}) async-done(((bf16[2048,512]{1,0:T(8,128)(2,1)}, bf16[2048,512]{1,0:T(8,128)(2,1)}, bf16[2048,512]{1,0:T(8,128)(2,1)}, bf16[2048,512]{1,0:T(8,128)(2,1)}), (bf16[2048,512]{1,0:T(8,128)(2,1)}, bf16[2048,512]{1,0:T(8,128)(2,1)}, ...) | async-done | bytes 8388624 | tf_op jit(solution)/shard_map/psum | solution.py:9
  220.3 12.8 %fusion = f32[512,2048]{0,1:T(8,128)} fusion(bf16[2048,512]{1,0:T(8,128)(2,1)} %get-tuple-element.44, bf16[2048,512]{1,0:T(8,128)(2,1)} %get-tuple-element.41, bf16[2048,512]{1,0:T(8,128)(2,1)} %get-tuple-element.42, bf16[2048,512]{1,0:T(8,128)(2,1)} %get-tuple-element.43, f32[2048]{0:T(1024)S(1)} %copy-done.4), kind=kOutput, calls=%fused_computation.5 | convolution fusion | flops 4336910336 | bytes 12591104 | tf_op jit(solution)/shard_map/sb,sc->bc/dot_general | solution.py:31
  233.7 34.0 %fusion.9 = f32[1536,4096]{0,1:T(8,128)} fusion(bf16[2048,4096]{1,0:T(8,128)(2,1)} %mul.69, f32[2048]{0:T(1024)S(1)} %copy-done.4, bf16[2048,512]{1,0:T(8,128)(2,1)} %get-tuple-element.41, bf16[2048,512]{1,0:T(8,128)(2,1)} %get-tuple-element.42, bf16[2048,512]{1,0:T(8,128)(2,1)} %get-tuple-element.43), kind=kOutput, calls=%fused_computation.14 | convolution fusion | flops 25813843968 | bytes 48242688 | tf_op jit(solution)/shard_map/sb,sc->bc/dot_general | solution.py:46
  267.7 15.7 %fusion.10 = f32[512,4096]{1,0:T(8,128)} fusion(bf16[2048,512]{1,0:T(8,128)(2,1)S(1)} %copy-done.3, bf16[2048,4096]{1,0:T(8,128)(2,1)} %mul.69, f32[2048]{0:T(1024)S(1)} %copy-done.4), kind=kOutput, calls=%fused_computation.15 | convolution fusion | flops 8615100416 | bytes 27271168 | tf_op jit(solution)/shard_map/sb,sc->bc/dot_general | solution.py:43
  283.5 53.6 %all-reduce.6.cloned.1.call-done = f32[512,2048]{0,1:T(8,128)} async-done(((f32[512,2048]{0,1:T(8,128)}), f32[512,2048]{0,1:T(8,128)}) %all-reduce.6.cloned.1.call-update) | async-done | bytes 4194320 | tf_op jit(solution)/shard_map/psum | solution.py:30
  337.1 1.4 slice_add_fusion
  338.8 1.5 fusion.20
  340.3 11.7 %cholesky.103 = f32[128,128]{1,0:T(8,128)S(1)} custom-call(f32[128,128]{1,0:T(8,128)S(1)} %cholesky.263), custom_call_target="Cholesky" | custom-call | tf_op jit(solution)/shard_map/jit(cholesky)/cholesky | solution.py:37
  352.0 9.8 %custom-call.31 = f32[1,128,128]{1,2,0:T(8,128)S(1)} custom-call(f32[1,128,128]{2,1,0:T(8,128)S(1)} %get-tuple-element.56), custom_call_target="InvertDiagBlocksLowerTriangular" | custom-call | tf_op jit(solution)/shard_map/jit(cholesky)/cholesky | solution.py:37
  362.5 11.7 %cholesky.215 = f32[128,128]{1,0:T(8,128)S(1)} custom-call(f32[128,128]{1,0:T(8,128)S(1)} %cholesky.267), custom_call_target="Cholesky" | custom-call | tf_op jit(solution)/shard_map/jit(cholesky)/cholesky | solution.py:37
  374.6 10.2 %custom-call.32 = f32[1,128,128]{1,2,0:T(8,128)S(1)} custom-call(f32[1,128,128]{2,1,0:T(8,128)S(1)} %get-tuple-element.54), custom_call_target="InvertDiagBlocksLowerTriangular" | custom-call | tf_op jit(solution)/shard_map/jit(cholesky)/cholesky | solution.py:37
  385.3 1.5 convolution_subtract_fusion.4
  386.8 11.7 %cholesky.236 = f32[128,128]{1,0:T(8,128)S(1)} custom-call(f32[128,128]{1,0:T(8,128)S(1)} %cholesky.272), custom_call_target="Cholesky" | custom-call | tf_op jit(solution)/shard_map/jit(cholesky)/cholesky | solution.py:37
  398.7 9.8 %custom-call.33 = f32[1,128,128]{1,2,0:T(8,128)S(1)} custom-call(f32[1,128,128]{2,1,0:T(8,128)S(1)} %get-tuple-element.52), custom_call_target="InvertDiagBlocksLowerTriangular" | custom-call | tf_op jit(solution)/shard_map/jit(cholesky)/cholesky | solution.py:37
  408.8 1.3 convolution_subtract_fusion.5
  410.1 11.9 %cholesky.253 = f32[128,128]{1,0:T(8,128)S(1)} custom-call(f32[128,128]{1,0:T(8,128)S(1)} %convolution_subtract_fusion.5), custom_call_target="Cholesky" | custom-call | tf_op jit(solution)/shard_map/jit(cholesky)/cholesky | solution.py:37
  426.7 10.7 %while.2 = (s32[]{:T(128)}, f32[512,512]{0,1:T(8,128)S(1)}, s32[4,2]{0,1:T(2,128)S(1)}, f32[4,128,128]{2,1,0:T(8,128)}, s32[]{:T(128)}) while((s32[]{:T(128)}, f32[512,512]{0,1:T(8,128)S(1)}, s32[4,2]{0,1:T(2,128)S(1)}, f32[4,128,128]{2,1,0:T(8,128)}, s32[]{:T(128)}) %tuple.32), condition=%wide.while_cond.1, body=%wide.while_body.1.sunk | while | flops 2 | bytes 393829 | solution.py:38
  427.4 1.3 dynamic-slice.15
  437.4 40.1 %custom-call.34 = f32[4,128,128]{1,2,0:T(8,128)S(1)} custom-call(f32[4,128,128]{2,1,0:T(8,128)} %get-tuple-element.24), custom_call_target="InvertDiagBlocksLowerTriangular" | custom-call | tf_op jit(solution)/shard_map/jit(_solve_triangular)/triangular_solve | solution.py:38
  481.2 1.5 convolution_subtract_fusion.2
  487.5 7.3 fusion.17
  494.8 7.2 fusion.16
  502.0 34.8 %pad_add_fusion = f32[2048,4096]{0,1:T(8,128)} fusion(f32[1536,4096]{0,1:T(8,128)} %fusion.9, f32[2048,512]{0,1:T(8,128)} %fusion.16, f32[512,4096]{1,0:T(8,128)} %fusion.10), kind=kOutput, calls=%fused_computation.2 | convolution fusion | flops 25778192384 | bytes 71303168 | tf_op jit(solution)/shard_map/dot_general | solution.py:49
  537.4 288.0 %reduce-scatter.2.cloned.1.call-done = f32[512,4096]{0,1:T(8,128)} async-done(((f32[2048,4096]{0,1:T(8,128)}), f32[512,4096]{0,1:T(8,128)}) %reduce-scatter.2.cloned.1.call-update) | async-done | bytes 8388624 | tf_op jit(solution)/shard_map/reduce_scatter | solution.py:51
  825.4 3.4 fusion.19
  828.9 10.4 %copy.40 = f32[512,8,512]{2,1,0:T(8,128)} copy(f32[512,8,512]{0,2,1:T(8,128)} %bitcast.66) | data formatting | bytes 16777216 | tf_op jit(solution)/shard_map/reshape | solution.py:59
  (84 shorter events, 25.0 us)
Async XLA Ops:
  6.5 213.8 %all-reduce.8.cloned.1.call-start = ((), (), s32[]{:S(2)}) async-start(), calls=%async_computation.3 | async-start | bytes 16777216 | tf_op jit(solution)/shard_map/psum | solution.py:9
  41.8 0.7 copy-start.2
  41.8 178.5 %copy-start.4 = (f32[2048]{0:T(1024)S(1)}, f32[2048]{0:T(1024)}, u32[]{:S(2)}) copy-start(f32[2048]{0:T(1024)} %param.7) | copy-start | bytes 24580
  41.9 295.2 %all-reduce.6.cloned.1.call-start = ((), (), s32[]{:S(2)}) async-start(), calls=%async_computation.1 | async-start | bytes 8388608 | tf_op jit(solution)/shard_map/psum | solution.py:30
  233.2 34.6 %copy-start.3 = (bf16[2048,512]{1,0:T(8,128)(2,1)S(1)}, bf16[2048,512]{1,0:T(8,128)(2,1)}, u32[]{:S(2)}) copy-start(bf16[2048,512]{1,0:T(8,128)(2,1)} %get-tuple-element.44) | copy-start | bytes 6291460
  233.2 592.3 %reduce-scatter.2.cloned.1.call-start = ((), (), s32[]{:S(2)}) async-start(), calls=%async_computation.2 | async-start | bytes 41943040 | tf_op jit(solution)/shard_map/reduce_scatter | solution.py:51
  340.3 34.4 %copy-start = (f32[512,512]{1,0:T(8,128)}, f32[512,512]{1,0:T(8,128)S(1)}, u32[]{:S(2)}) copy-start(f32[512,512]{1,0:T(8,128)S(1)} %fusion.20) | copy-start | bytes 3145732
  477.6 0.9 copy-start.1
Sparse Core Ops, SparseCore 0:
  42.0 178.3 all-reduce.7
  233.3 103.7 all-reduce.5
  536.9 288.5 reduce-scatter.1
where the time goes:
time: 853 us; the launch traced here: 846 us
  waiting for transfers between devices  510 us (60%)
  other arithmetic  141 us (17%)
  matrix products  122 us (14%)
  local copies, waits for them, and re-layouts  46.3 us (5%)
  between operations  16.2 us (2%)
  blocking collectives  9.56 us (1%)
    reduce_scatter x1, waiting for transfers between devices, body(): result = lax.psum_scatter(partial, 'row', scatter_dimension=0, tiled=True)  288 us
    psum x1, waiting for transfers between devices, spread(): return lax.psum(jnp.where(mine, value, jnp.zeros_like(value)), axis)  168 us
    another operation x14, other arithmetic, body(): lower = jnp.linalg.cholesky(corner)  78.9 us
    psum x1, waiting for transfers between devices, body(): lax.psum(jnp.einsum('sb,sc->bc', band[:, :tile], band_weighted, preferred...  53.6 us
    another operation x3, other arithmetic, body(): lower_inv = jax.scipy.linalg.solve_triangular(lower, identity, lower=True)  40.3 us
    dot_general x1, matrix products, body(): moved = jnp.dot(transform, part_head, precision=lax.Precision.HIGH)  34.8 us
    dot_general x1, matrix products, body(): jnp.einsum('sb,sc->bc', band[:, tile:], weighted, preferred_element_type=...  34 us
    unnamed x17, local copies, waits for them, and re-layouts  22 us
  transfers between devices with their start and end apart: 3, of which 3 were waited for; matrix products, arithmetic and copies ran while one was open for 6% of the time, Pallas kernels for 0%

commit v1 on v0

--- a/solution.py
+++ b/solution.py
@@ -4,9 +4,13 @@
 from jax.sharding import PartitionSpec as P
 
 
+def _mark_weights(mine_x, lane_axis):
+    return jnp.sum(lax.all_gather(mine_x, lane_axis), axis=0)
+
+
 def spread(value, axis, root):
     mine = lax.axis_index(axis) == root
-    return lax.psum(jnp.where(mine, value, jnp.zeros_like(value)), axis)
+    return _mark_weights(jnp.where(mine, value, jnp.zeros_like(value)), axis)
 
 
 def body(sensitivity, sample_weight, pattern, prior):

time: 853 us -> 1290 us (1.51)
  waiting for transfers between devices: 510 us -> 905 us
  other arithmetic: 141 us -> 183 us
    all_gather x0 -> x4, waiting for transfers between devices: none -> 563 us  [_mark_weights(): return jnp.sum(lax.all_gather(mine_x, lane_axis), axis=0)]
    psum x1 -> x0, waiting for transfers between devices: 168 us -> none  [spread(): return lax.psum(jnp.where(mine, value, jnp.zeros_like(value)), axis)]
    reduce_sum x0 -> x4, other arithmetic: none -> 42 us  [_mark_weights(): return jnp.sum(lax.all_gather(mine_x, lane_axis), axis=0)]
  transfers between devices with their start and end apart: 3 -> 6, of which waited for: 3 -> 6; matrix products, arithmetic and copies ran while one was open for 6% -> 6% of each run, Pallas kernels for 0% -> 0%
where the time goes in v1:
time: 1290 us; the launch traced here: 1280 us
  waiting for transfers between devices  905 us (70%)
  other arithmetic  183 us (14%)
  matrix products  120 us (9%)
  local copies, waits for them, and re-layouts  45.7 us (4%)
  between operations  16.7 us (1%)
    all_gather x4, waiting for transfers between devices, _mark_weights(): return jnp.sum(lax.all_gather(mine_x, lane_axis), axis=0)  563 us
    reduce_scatter x1, waiting for transfers between devices, body(): result = lax.psum_scatter(partial, 'row', scatter_dimension=0, tiled=True)  288 us
    another operation x14, other arithmetic, body(): lower = jnp.linalg.cholesky(corner)  78.9 us
    psum x1, waiting for transfers between devices, body(): lax.psum(jnp.einsum('sb,sc->bc', band[:, :tile], band_weighted, preferred...  51.5 us
    reduce_sum x4, other arithmetic, _mark_weights(): return jnp.sum(lax.all_gather(mine_x, lane_axis), axis=0)  42 us
    another operation x3, other arithmetic, body(): lower_inv = jax.scipy.linalg.solve_triangular(lower, identity, lower=True)  40.3 us
    dot_general x1, matrix products, body(): jnp.einsum('sb,sc->bc', band[:, tile:], weighted, preferred_element_type=...  34.8 us
    dot_general x1, matrix products, body(): moved = jnp.dot(transform, part_head, precision=lax.Precision.HIGH)  34.8 us
  transfers between devices with their start and end apart: 6, of which 6 were waited for; matrix products, arithmetic and copies ran while one was open for 6% of the time, Pallas kernels for 0%

profile of v1, /device:TPU:0, one launch (start us, length us, event | category | flops | bytes accessed | tf_op | source)
XLA Modules:
  0.0 1280.9 jit_solution(15716190443234742049)
XLA Ops:
  9.0 6.3 copy.50
  15.2 12.2 copy.49
  27.4 9.4 mul.69
  36.8 5.1 broadcast_select_fusion.3
  44.0 9.6 all-gather.4
  53.8 142.0 %all-gather.10.cloned.1.call-done = bf16[16384,512]{1,0:T(8,128)(2,1)} async-done(((bf16[2048,512]{1,0:T(8,128)(2,1)}), bf16[16384,512]{1,0:T(8,128)(2,1)}) %all-gather.10.cloned.1.call-update) | async-done | bytes 16777232 | tf_op jit(solution)/shard_map/all_gather | solution.py:8
  195.8 9.6 reduce_sum.48
  205.4 141.3 %all-gather.12.cloned.1.call-done = bf16[16384,512]{1,0:T(8,128)(2,1)} async-done(((bf16[2048,512]{1,0:T(8,128)(2,1)}), bf16[16384,512]{1,0:T(8,128)(2,1)}) %all-gather.12.cloned.1.call-update) | async-done | bytes 16777232 | tf_op jit(solution)/shard_map/all_gather | solution.py:8
  346.7 10.9 reduce_sum.49
  357.6 140.0 %all-gather.14.cloned.1.call-done = bf16[16384,512]{1,0:T(8,128)(2,1)} async-done(((bf16[2048,512]{1,0:T(8,128)(2,1)}), bf16[16384,512]{1,0:T(8,128)(2,1)}) %all-gather.14.cloned.1.call-update) | async-done | bytes 16777232 | tf_op jit(solution)/shard_map/all_gather | solution.py:8
  497.6 11.0 reduce_sum.50
  508.6 139.7 %all-gather.16.cloned.1.call-done = bf16[16384,512]{1,0:T(8,128)(2,1)} async-done(((bf16[2048,512]{1,0:T(8,128)(2,1)}), bf16[16384,512]{1,0:T(8,128)(2,1)}) %all-gather.16.cloned.1.call-update) | async-done | bytes 16777232 | tf_op jit(solution)/shard_map/all_gather | solution.py:8
  648.4 10.5 reduce_sum.51
  658.9 10.6 fusion
  670.0 34.8 %fusion.9 = f32[1536,4096]{0,1:T(8,128)} fusion(bf16[2048,4096]{1,0:T(8,128)(2,1)} %mul.69, f32[2048]{0:T(1024)S(1)} %copy-done.3, bf16[2048,512]{1,0:T(8,128)(2,1)} %reduce_sum.51, bf16[2048,512]{1,0:T(8,128)(2,1)} %reduce_sum.50, bf16[2048,512]{1,0:T(8,128)(2,1)} %reduce_sum.49), kind=kOutput, calls=%fused_computation.14 | convolution fusion | flops 25813843968 | bytes 48242688 | tf_op jit(solution)/shard_map/sb,sc->bc/dot_general | solution.py:50
  704.8 15.1 %fusion.10 = f32[512,4096]{1,0:T(8,128)} fusion(bf16[2048,512]{1,0:T(8,128)(2,1)S(1)} %reduce_sum.48, bf16[2048,4096]{1,0:T(8,128)(2,1)} %mul.69, f32[2048]{0:T(1024)S(1)} %copy-done.3), kind=kOutput, calls=%fused_computation.15 | convolution fusion | flops 8615100416 | bytes 27271168 | tf_op jit(solution)/shard_map/sb,sc->bc/dot_general | solution.py:47
  719.9 51.5 %all-reduce.4.cloned.1.call-done = f32[512,2048]{0,1:T(8,128)} async-done(((f32[512,2048]{0,1:T(8,128)}), f32[512,2048]{0,1:T(8,128)}) %all-reduce.4.cloned.1.call-update) | async-done | bytes 4194320 | tf_op jit(solution)/shard_map/psum | solution.py:34
  774.7 11.7 cholesky.103
  786.5 9.8 custom-call.31
  796.9 11.7 cholesky.215
  809.0 10.2 custom-call.32
  821.2 11.7 cholesky.236
  833.1 9.8 custom-call.33
  844.5 11.9 cholesky.253
  861.2 10.7 while.2
  871.9 40.1 %custom-call.34 = f32[4,128,128]{1,2,0:T(8,128)S(1)} custom-call(f32[4,128,128]{2,1,0:T(8,128)} %get-tuple-element.24), custom_call_target="InvertDiagBlocksLowerTriangular" | custom-call | tf_op jit(solution)/shard_map/jit(_solve_triangular)/triangular_solve | solution.py:42
  921.9 7.3 fusion.17
  929.2 7.2 fusion.16
  936.4 34.8 %pad_add_fusion = f32[2048,4096]{0,1:T(8,128)} fusion(f32[1536,4096]{0,1:T(8,128)} %fusion.9, f32[2048,512]{0,1:T(8,128)} %fusion.16, f32[512,4096]{1,0:T(8,128)} %fusion.10), kind=kOutput, calls=%fused_computation.2 | convolution fusion | flops 25778192384 | bytes 71303168 | tf_op jit(solution)/shard_map/dot_general | solution.py:53
  971.8 288.0 %reduce-scatter.2.cloned.1.call-done = f32[512,4096]{0,1:T(8,128)} async-done(((f32[2048,4096]{0,1:T(8,128)}), f32[512,4096]{0,1:T(8,128)}) %reduce-scatter.2.cloned.1.call-update) | async-done | bytes 8388624 | tf_op jit(solution)/shard_map/reduce_scatter | solution.py:55
  1259.9 3.4 fusion.19
  1263.3 10.4 copy.40
  (95 shorter events, 36.6 us)
Async XLA Ops:
  6.5 189.3 %all-gather.10.cloned.1.call-start = ((), (), s32[]{:S(2)}) async-start(), calls=%async_computation.3 | async-start | bytes 18874368 | tf_op jit(solution)/shard_map/all_gather | solution.py:8
  41.8 2.1 copy-start.2
  41.9 304.9 %all-gather.12.cloned.1.call-start = ((), (), s32[]{:S(2)}) async-start(), calls=%async_computation.4 | async-start | bytes 18874368 | tf_op jit(solution)/shard_map/all_gather | solution.py:8
  42.6 455.0 %all-gather.14.cloned.1.call-start = ((), (), s32[]{:S(2)}) async-start(), calls=%async_computation.5 | async-start | bytes 18874368 | tf_op jit(solution)/shard_map/all_gather | solution.py:8
  43.3 605.0 %all-gather.16.cloned.1.call-start = ((), (), s32[]{:S(2)}) async-start(), calls=%async_computation.6 | async-start | bytes 18874368 | tf_op jit(solution)/shard_map/all_gather | solution.py:8
  43.9 727.6 %all-reduce.4.cloned.1.call-start = ((), (), s32[]{:S(2)}) async-start(), calls=%async_computation.1 | async-start | bytes 8388608 | tf_op jit(solution)/shard_map/psum | solution.py:34
  648.4 10.5 copy-start.3
  669.5 590.3 %reduce-scatter.2.cloned.1.call-start = ((), (), s32[]{:S(2)}) async-start(), calls=%async_computation.2 | async-start | bytes 41943040 | tf_op jit(solution)/shard_map/reduce_scatter | solution.py:55
  774.7 34.4 %copy-start = (f32[512,512]{1,0:T(8,128)}, f32[512,512]{1,0:T(8,128)S(1)}, u32[]{:S(2)}) copy-start(f32[512,512]{1,0:T(8,128)S(1)} %fusion.20) | copy-start | bytes 3145732
  912.0 0.9 copy-start.1
Sparse Core Ops, SparseCore 0:
  42.0 153.7 all-gather.9
  197.4 149.2 all-gather.11
  348.3 149.2 all-gather.13
  499.1 149.2 all-gather.15
  669.6 101.7 all-reduce.3
  971.3 288.5 reduce-scatter.1
